TPU v7x, 128 devices: a whole 4x4x4 slice. The times are simulated.
128 devices in a mesh: rows: 32 (over y, x, core), rep: 4 (over z).
Axes of the slice: x: 4, y: 4, z: 4, core: 2. Of those that a mesh axis runs over, the one named last changes fastest.
Arguments:
- weights: bfloat16 [80, 2097152], P('rep', 'rows'), may hold values from 0.25 to 4
- cell_ids: int32 [2097152], P('rows'), may hold values from 0 to 31
- group_sizes: int32 [32, 1024], P('rows'), may hold values from 32 to 96, as said below
- group_county: int32 [32768, 1], P('rows'), may hold values from 0 to 1023; in each aligned block of 1024 rows (0 to 1023, 1024 to 2047, ...) at most 2 rows name the same one
- age_rate: float32 [1024, 4], P('rows'), may hold values from 8 to 40
- kind_rate: float32 [1024, 8], P('rows'), may hold values from 2 to 20
Outputs:
- raked: float32 [32768, 2560], P('rows', 'rep')
- spread: float32 [32768, 32], P('rows')
Inputs may be any that keep to these rules, and one draw needn't show every extreme that they name: `group_sizes`: each shard's 1024 sizes sum to 65536. `group_county`: among the 1024 block groups of one shard, no county holds more than 2.
All inputs are finite; a program needn't handle non-finite values.
Results may differ from a plain program's by a relative error of at most 0.0003.
Values sent between devices are 32-bit elements; how exact they have to be, the bound alone decides.
No kernel may reach another device: no remote copies, remote signals or barrier semaphores. Data moves between devices by JAX's collectives and lax.ppermute only.
A program may use at most 64 MiB of HBM per device.

v0:
```python
import jax
import jax.numpy as jnp
from jax import lax
from jax.sharding import PartitionSpec as P

AGES = 4
KINDS = 8
CELLS = 32
LOW = 32
ITERS = 4


def rake(county_tables, groups_in, age_rate, kind_rate):
    county_rows = county_tables.shape[0]
    current = county_tables.reshape(county_rows, -1, AGES, KINDS)
    age_goal = (age_rate * groups_in[:, None])[:, None, :]
    kind_goal = (kind_rate * groups_in[:, None])[:, None, :]
    factor = jnp.ones_like(current)
    for sweep_index in range(ITERS):
        ratios = age_goal / jnp.maximum(jnp.sum(current, axis=3), 1.0)
        current = current * ratios[:, :, :, None]
        factor = factor * ratios[:, :, :, None]
        ratios = kind_goal / jnp.maximum(jnp.sum(current, axis=2), 1.0)
        current = current * ratios[:, :, None, :]
        factor = factor * ratios[:, :, None, :]
    return factor.reshape(county_rows, -1)


def exact_dot(left, right):
    return jnp.dot(left, right, precision=lax.Precision.HIGHEST, preferred_element_type=jnp.float32)


def tabulate(weights, cell_ids, group_sizes):
    reps_here, records_here = weights.shape
    group_here = group_sizes.shape[1]
    row_width = reps_here * CELLS
    block_rows = min(4096, records_here)
    window = block_rows // LOW + 2
    group_range = jnp.arange(group_here, dtype=jnp.int32)
    upper = (group_range[:, None] <= group_range[None, :]).astype(jnp.float32)
    sizes_float = group_sizes.astype(jnp.float32)
    group_ends = exact_dot(sizes_float, upper)[0].astype(jnp.int32)
    group_starts = group_ends - group_sizes[0]
    beyond = jnp.full((window,), records_here + 1, jnp.int32)
    ends_padded = jnp.concatenate([group_ends, beyond])
    starts_padded = jnp.concatenate([group_starts, beyond])
    cell_range = jnp.arange(CELLS, dtype=jnp.int32)
    block_range = jnp.arange(block_rows, dtype=jnp.int32)

    def add_block(block_index, totals):
        start = block_index * block_rows
        weight_block = lax.dynamic_slice_in_dim(weights, start, block_rows, 1)
        cell_block = lax.dynamic_slice_in_dim(cell_ids, start, block_rows, 0)
        first_slot = jnp.sum((group_ends <= start).astype(jnp.int32))
        ends_window = lax.dynamic_slice_in_dim(ends_padded, first_slot, window, 0)
        starts_window = lax.dynamic_slice_in_dim(starts_padded, first_slot, window, 0)
        place = start + block_range
        slot_hot = (
            (place[:, None] >= starts_window[None, :]) & (place[:, None] < ends_window[None, :])
        ).astype(jnp.bfloat16)
        cell_hot = (cell_block[None, None, :] == cell_range[None, :, None]).astype(jnp.bfloat16)
        spread_cells = (weight_block[:, None, :] * cell_hot).reshape(row_width, block_rows)
        product = jnp.dot(spread_cells, slot_hot, preferred_element_type=jnp.float32)
        current = lax.dynamic_slice_in_dim(totals, first_slot, window, 1)
        return lax.dynamic_update_slice_in_dim(totals, current + product, first_slot, 1)

    totals = jnp.zeros((row_width, group_here + window), jnp.float32)
    totals = lax.fori_loop(0, records_here // block_rows, add_block, totals)
    return totals[:, :group_here].T


def local(weights, cell_ids, group_sizes, group_county, age_rate, kind_rate):
    tables = tabulate(weights, cell_ids, group_sizes)
    group_here, row_width = tables.shape
    county_ids = group_county[:, 0]
    owners = lax.axis_size("rows")
    county_here = age_rate.shape[0]
    counties = county_here * owners
    pair_slots = max(2, 5 * group_here // (2 * counties))
    same_county = county_ids[:, None] == county_ids[None, :]
    group_order = jnp.arange(group_here, dtype=jnp.int32)
    earlier = group_order[:, None] > group_order[None, :]
    rank_within = jnp.sum((same_county & earlier).astype(jnp.int32), axis=1)
    slot_index = county_ids * pair_slots + rank_within
    slot_range = jnp.arange(counties * pair_slots, dtype=jnp.int32)
    slot_hot = (slot_index[:, None] == slot_range[None, :]).astype(jnp.float32)
    outgoing = exact_dot(slot_hot.T, tables).reshape(counties, pair_slots, row_width)
    present = jnp.sum(slot_hot, axis=0).reshape(counties, pair_slots)
    arrived, arrived_flags = (
        lax.all_to_all(outgoing, "rows", split_axis=0, concat_axis=1, tiled=True),
        lax.all_to_all(present, "rows", split_axis=0, concat_axis=1, tiled=True),
    )
    factor = rake(jnp.sum(arrived, axis=1), jnp.sum(arrived_flags, axis=1), age_rate, kind_rate)
    returned = lax.all_to_all(
        arrived * factor[:, None, :], "rows", split_axis=1, concat_axis=0, tiled=True
    )
    raked = exact_dot(slot_hot, returned.reshape(counties * pair_slots, row_width))
    reps_here = row_width // CELLS
    shaped = raked.reshape(group_here, reps_here, CELLS)
    total_reps = reps_here * lax.axis_size("rep")
    centre = lax.psum(jnp.sum(shaped, axis=1), "rep") / total_reps
    deviation = lax.psum(jnp.sum(jnp.square(shaped - centre[:, None, :]), axis=1), "rep")
    return (raked, deviation * (4.0 / total_reps))


def solution(mesh):
    placed = (
        P("rep", "rows"),
        P("rows"),
        P("rows", None),
        P("rows", None),
        P("rows", None),
        P("rows", None),
    )
    return jax.shard_map(
        local,
        mesh=mesh,
        in_specs=placed,
        out_specs=(P("rows", "rep"), P("rows", None)),
        check_vma=False,
    )
```

profile of v0, /device:TPU:0, one launch (start us, length us, event | category | flops | bytes accessed | tf_op | source)
XLA Modules:
  0.0 535.9 jit_solution(4150225946074218056)
XLA Ops:
  11.5 7.6 %all-to-all-start.1 = ((f32[32,32,2]{1,2,0:T(2,128)}), f32[32,32,2]{1,2,0:T(2,128)S(1)}, u32[]{:S(2)}, u32[]{:S(2)}) async-start(f32[32,32,2]{1,2,0:T(2,128)} %copy.28), calls=%async_computation.1 | async-start | bytes 65536 | tf_op jit(solution)/shard_map/all_to_all | solution.py:91
  21.4 216.4 %while.14 = (s32[]{:T(128)}, f32[640,1154]{0,1:T(8,128)S(1)}, s32[1024]{0:T(1024)S(1)}, bf16[20,65536]{1,0:T(8,128)(2,1)}, s32[65536]{0:T(1024)}, /*index=5*/s32...) while((s32[]{:T(128)}, f32[640,1154]{0,1:T(8,128)S(1)}, ...), condition=%wide.region_3.0_spmd.clone, body=%wide.region_1.3_spmd.clone.sunk | while | flops 686145792 | bytes 12922137 | solution.py:68
  28.6 4.3 fusion.35
  55.7 4.3 fusion.35
  69.2 4.3 fusion.35
  82.7 4.3 fusion.35
  109.8 4.3 fusion.35
  136.8 4.3 fusion.35
  163.9 4.3 fusion.35
  190.9 4.3 fusion.35
  218.0 4.3 fusion.35
  231.5 4.3 fusion.35
  237.8 13.5 %fusion.16 = f32[2048,640]{1,0:T(8,128)} fusion(s32[1024]{0:T(1024)S(1)} %bitcast.49, f32[640,1154]{0,1:T(8,128)S(1)} %get-tuple-element.156), kind=kOutput, calls=%fused_computation.19 | convolution fusion | flops 16108224512 | bytes 7868416 | tf_op jit(solution)/shard_map/dot_general | solution.py:30
  251.3 7.4 %reshape.177 = f32[1024,2,640]{2,1,0:T(2,128)} reshape(f32[2048,640]{1,0:T(8,128)} %fusion.16) | data formatting | bytes 10485760 | tf_op jit(solution)/shard_map/reshape | solution.py:87
  258.7 7.5 %all-to-all-start = ((f32[1024,2,640]{2,1,0:T(2,128)}), f32[1024,2,640]{2,1,0:T(2,128)}, u32[]{:S(2)}, u32[]{:S(2)}) async-start(f32[1024,2,640]{2,1,0:T(2,128)} %reshape.177), calls=%async_computation | async-start | bytes 10485760 | tf_op jit(solution)/shard_map/all_to_all | solution.py:90
  266.5 65.5 %all-to-all-done = f32[1024,2,640]{2,1,0:T(2,128)} async-done(((f32[1024,2,640]{2,1,0:T(2,128)}), f32[1024,2,640]{2,1,0:T(2,128)}, u32[]{:S(2)}, u32[]{:S(2)}) %all-to-all-start) | async-done | bytes 5242912 | tf_op jit(solution)/shard_map/all_to_all | solution.py:90
  332.0 5.2 copy.26
  339.9 5.3 copy.27
  349.8 65.2 %all_to_all.46 = f32[32,64,640]{2,0,1:T(8,128)S(1)} all-to-all(f32[32,64,640]{2,0,1:T(8,128)S(1)} %bitcast_multiply_fusion), channel_id=1, replica_groups=mesh['rows'=32,'rep'=4] {'rows'}, dimensions={1} | all-to-all | bytes 10485760 | tf_op jit(solution)/shard_map/all_to_all | solution.py:94
  415.0 6.4 %copy.34 = f32[32,32,2,640]{3,2,0,1:T(2,128)} copy(f32[32,32,2,640]{3,0,2,1:T(8,128)S(1)} %bitcast.41) | data formatting | bytes 10485760 | tf_op jit(solution)/shard_map/all_to_all | solution.py:94
  421.4 7.6 %reshape.179 = f32[2048,640]{1,0:T(8,128)} reshape(f32[32,32,2,640]{3,2,1,0:T(2,128)} %bitcast.42) | data formatting | bytes 10485760 | tf_op jit(solution)/shard_map/reshape | solution.py:97
  429.0 11.2 %fusion.15 = f32[1024,640]{0,1:T(8,128)S(1)} fusion(f32[2048,640]{1,0:T(8,128)} %reshape.179, s32[1024]{0:T(1024)S(1)} %bitcast.50), kind=kOutput, calls=%fused_computation.18 | convolution fusion | flops 16108224512 | bytes 7868416 | tf_op jit(solution)/shard_map/dot_general | solution.py:30
  441.1 41.5 %all-reduce.5.cloned.1.call-done = f32[1024,32]{0,1:T(8,128)} async-done(((f32[1024,32]{0,1:T(8,128)}), f32[1024,32]{0,1:T(8,128)}) %all-reduce.5.cloned.1.call-update) | async-done | bytes 131088 | tf_op jit(solution)/shard_map/psum | solution.py:101
  486.6 40.9 %all-reduce.7.cloned.1.call-done = f32[1024,32]{0,1:T(8,128)} async-done(((f32[1024,32]{0,1:T(8,128)}), f32[1024,32]{0,1:T(8,128)}) %all-reduce.7.cloned.1.call-update) | async-done | bytes 131088 | tf_op jit(solution)/shard_map/psum | solution.py:102
  (199 shorter events, 162.4 us)
Async XLA Ops:
  11.5 247.1 %all-to-all-start.1 = ((f32[32,32,2]{1,2,0:T(2,128)}), f32[32,32,2]{1,2,0:T(2,128)S(1)}, u32[]{:S(2)}, u32[]{:S(2)}) async-start(f32[32,32,2]{1,2,0:T(2,128)} %copy.28), calls=%async_computation.1 | async-start | bytes 65536 | tf_op jit(solution)/shard_map/all_to_all | solution.py:91
  258.7 7.8 %copy-start.1 = (f32[32,4]{0,1:T(4,128)S(1)}, f32[32,4]{0,1:T(4,128)}, u32[]{:S(2)}) copy-start(f32[32,4]{0,1:T(4,128)} %param.12) | copy-start | bytes 1540
  258.7 7.8 %copy-start = (f32[32,8]{0,1:T(8,128)S(1)}, f32[32,8]{0,1:T(8,128)}, u32[]{:S(2)}) copy-start(f32[32,8]{0,1:T(8,128)} %param.13) | copy-start | bytes 3076
  258.7 73.4 %all-to-all-start = ((f32[1024,2,640]{2,1,0:T(2,128)}), f32[1024,2,640]{2,1,0:T(2,128)}, u32[]{:S(2)}, u32[]{:S(2)}) async-start(f32[1024,2,640]{2,1,0:T(2,128)} %reshape.177), calls=%async_computation | async-start | bytes 10485760 | tf_op jit(solution)/shard_map/all_to_all | solution.py:90
  266.1 216.4 %all-reduce.5.cloned.1.call-start = ((), (), s32[]{:S(2)}) async-start(), calls=%async_computation.3 | async-start | bytes 262144 | tf_op jit(solution)/shard_map/psum | solution.py:101
  441.0 86.5 %all-reduce.7.cloned.1.call-start = ((), (), s32[]{:S(2)}) async-start(), calls=%async_computation.4 | async-start | bytes 262144 | tf_op jit(solution)/shard_map/psum | solution.py:102
Sparse Core Ops, SparseCore 0:
  441.1 41.3 all-reduce.4
  485.4 41.9 all-reduce.6
where the time goes:
time: 539 us; the launch traced here: 536 us
  waiting for transfers between devices  148 us (27%)
  local copies, waits for them, and re-layouts  95.7 us (18%)
  matrix products  95.4 us (18%)
  other arithmetic  70.8 us (13%)
  blocking collectives  65.2 us (12%)
  loops' own time  31.2 us (6%)
  starting transfers between devices  15.4 us (3%)
  between operations  14.2 us (3%)
    dot_general x16, matrix products, add_block(): jnp.dot(spread_cells, slot_hot, preferred_element_type=jnp.float32)  69.4 us
    all_to_all x1, waiting for transfers between devices, local(): lax.all_to_all(outgoing, 'rows', split_axis=0, concat_axis=1, tiled=True)  65.5 us
    all_to_all x1, blocking collectives, local(): lax.all_to_all(arrived * factor[:, None, :], 'rows', split_axis=1, concat...  65.2 us
    mul x16, other arithmetic, add_block(): weight_block[:, None, :] * cell_hot  44.4 us
    psum x1, waiting for transfers between devices, local(): centre = lax.psum(jnp.sum(shaped, axis=1), 'rep') / total_reps  41.5 us
    psum x1, waiting for transfers between devices, local(): lax.psum(jnp.sum(jnp.square(shaped - centre[:, None, :]), axis=1), 'rep')  40.9 us
    another operation x1, loops' own time, tabulate(): totals = lax.fori_loop(0, records_here // block_rows, add_block, totals)  31.2 us
    dynamic_update_slice x16, local copies, waits for them, and re-layouts, add_block(): lax.dynamic_update_slice_in_dim(totals, current + product, first_slot, 1)  30.8 us
  transfers between devices with their start and end apart: 4, of which 3 were waited for; matrix products, arithmetic and copies ran while one was open for 39% of the time, Pallas kernels for 0%

commit v1 on v0

--- a/solution.py
+++ b/solution.py
@@ -99,7 +99,9 @@
     shaped = raked.reshape(group_here, reps_here, CELLS)
     total_reps = reps_here * lax.axis_size("rep")
     centre = lax.psum(jnp.sum(shaped, axis=1), "rep") / total_reps
-    deviation = lax.psum(jnp.sum(jnp.square(shaped - centre[:, None, :]), axis=1), "rep")
+    deviation = jnp.sum(
+        lax.all_gather(jnp.sum(jnp.square(shaped - centre[:, None, :]), axis=1), "rep"), axis=0
+    )
     return (raked, deviation * (4.0 / total_reps))
 
 

time: 539 us -> 508 us (0.942)
  waiting for transfers between devices: 148 us -> 105 us
  blocking collectives: 65.2 us -> 78 us
    psum x1 -> x0, waiting for transfers between devices: 40.9 us -> none  [local(): lax.psum(jnp.sum(jnp.square(shaped - centre[:, None, :]), axis=1), 'rep')]
    all_gather x0 -> x1, blocking collectives: none -> 12.8 us  [local(): lax.all_gather(jnp.sum(jnp.square(shaped - centre[:, None, :]), axis=1),...]
  transfers between devices with their start and end apart: 4 -> 3, of which waited for: 3 -> 2; matrix products, arithmetic and copies ran while one was open for 39% -> 42% of each run, Pallas kernels for 0% -> 0%
where the time goes in v1:
time: 508 us; the launch traced here: 505 us
  waiting for transfers between devices  105 us (21%)
  local copies, waits for them, and re-layouts  96.1 us (19%)
  matrix products  95.4 us (19%)
  blocking collectives  78 us (15%)
  other arithmetic  69.5 us (14%)
  loops' own time  31.2 us (6%)
  starting transfers between devices  15.3 us (3%)
  between operations  14.2 us (3%)
    dot_general x16, matrix products, add_block(): jnp.dot(spread_cells, slot_hot, preferred_element_type=jnp.float32)  69.4 us
    all_to_all x1, waiting for transfers between devices, local(): lax.all_to_all(outgoing, 'rows', split_axis=0, concat_axis=1, tiled=True)  65.5 us
    all_to_all x1, blocking collectives, local(): lax.all_to_all(arrived * factor[:, None, :], 'rows', split_axis=1, concat...  65.2 us
    mul x16, other arithmetic, add_block(): weight_block[:, None, :] * cell_hot  44.4 us
    psum x1, waiting for transfers between devices, local(): centre = lax.psum(jnp.sum(shaped, axis=1), 'rep') / total_reps  39.5 us
    another operation x1, loops' own time, tabulate(): totals = lax.fori_loop(0, records_here // block_rows, add_block, totals)  31.2 us
    dynamic_update_slice x16, local copies, waits for them, and re-layouts, add_block(): lax.dynamic_update_slice_in_dim(totals, current + product, first_slot, 1)  30.8 us
    dot_general x3, matrix products, exact_dot(): jnp.dot(left, right, precision=lax.Precision.HIGHEST, preferred_element_t...  26 us
  transfers between devices with their start and end apart: 3, of which 2 were waited for; matrix products, arithmetic and copies ran while one was open for 42% of the time, Pallas kernels for 0%

profile of v1, /device:TPU:0, one launch (start us, length us, event | category | flops | bytes accessed | tf_op | source)
XLA Modules:
  0.0 504.8 jit_solution(11302339075807324062)
XLA Ops:
  11.5 7.6 %all-to-all-start.1 = ((f32[32,32,2]{1,2,0:T(2,128)}), f32[32,32,2]{1,2,0:T(2,128)S(1)}, u32[]{:S(2)}, u32[]{:S(2)}) async-start(f32[32,32,2]{1,2,0:T(2,128)} %copy.28), calls=%async_computation.1 | async-start | bytes 65536 | tf_op jit(solution)/shard_map/all_to_all | solution.py:91
  21.4 216.4 %while.14 = (s32[]{:T(128)}, f32[640,1154]{0,1:T(8,128)S(1)}, s32[1024]{0:T(1024)S(1)}, bf16[20,65536]{1,0:T(8,128)(2,1)}, s32[65536]{0:T(1024)}, /*index=5*/s32...) while((s32[]{:T(128)}, f32[640,1154]{0,1:T(8,128)S(1)}, ...), condition=%wide.region_3.0_spmd.clone, body=%wide.region_1.3_spmd.clone.sunk | while | flops 686145792 | bytes 12922137 | solution.py:68
  28.6 4.3 fusion.35
  55.7 4.3 fusion.35
  69.2 4.3 fusion.35
  82.7 4.3 fusion.35
  109.8 4.3 fusion.35
  136.8 4.3 fusion.35
  163.9 4.3 fusion.35
  190.9 4.3 fusion.35
  218.0 4.3 fusion.35
  231.5 4.3 fusion.35
  237.8 13.5 %fusion.16 = f32[2048,640]{1,0:T(8,128)} fusion(s32[1024]{0:T(1024)S(1)} %bitcast.51, f32[640,1154]{0,1:T(8,128)S(1)} %get-tuple-element.156), kind=kOutput, calls=%fused_computation.19 | convolution fusion | flops 16108224512 | bytes 7868416 | tf_op jit(solution)/shard_map/dot_general | solution.py:30
  251.3 7.4 %reshape.177 = f32[1024,2,640]{2,1,0:T(2,128)} reshape(f32[2048,640]{1,0:T(8,128)} %fusion.16) | data formatting | bytes 10485760 | tf_op jit(solution)/shard_map/reshape | solution.py:87
  258.7 7.5 %all-to-all-start = ((f32[1024,2,640]{2,1,0:T(2,128)}), f32[1024,2,640]{2,1,0:T(2,128)}, u32[]{:S(2)}, u32[]{:S(2)}) async-start(f32[1024,2,640]{2,1,0:T(2,128)} %reshape.177), calls=%async_computation | async-start | bytes 10485760 | tf_op jit(solution)/shard_map/all_to_all | solution.py:90
  266.5 65.5 %all-to-all-done = f32[1024,2,640]{2,1,0:T(2,128)} async-done(((f32[1024,2,640]{2,1,0:T(2,128)}), f32[1024,2,640]{2,1,0:T(2,128)}, u32[]{:S(2)}, u32[]{:S(2)}) %all-to-all-start) | async-done | bytes 5242912 | tf_op jit(solution)/shard_map/all_to_all | solution.py:90
  332.0 5.2 %copy.26 = f32[1024,2,640]{2,0,1:T(8,128)} copy(f32[1024,2,640]{2,1,0:T(2,128)} %all-to-all-done) | data formatting | bytes 10485760 | tf_op jit(solution)/shard_map/all_to_all | solution.py:90
  339.9 5.3 %copy.27 = f32[32,32,2,640]{3,0,2,1:T(8,128)} copy(f32[32,32,2,640]{3,0,1,2:T(8,128)} %bitcast.32) | data formatting | bytes 10485760 | tf_op jit(solution)/shard_map/all_to_all | solution.py:90
  349.8 65.2 %all_to_all.46 = f32[32,64,640]{2,0,1:T(8,128)S(1)} all-to-all(f32[32,64,640]{2,0,1:T(8,128)S(1)} %bitcast_multiply_fusion), channel_id=1, replica_groups=mesh['rows'=32,'rep'=4] {'rows'}, dimensions={1} | all-to-all | bytes 10485760 | tf_op jit(solution)/shard_map/all_to_all | solution.py:94
  415.0 6.4 %copy.34 = f32[32,32,2,640]{3,2,0,1:T(2,128)} copy(f32[32,32,2,640]{3,0,2,1:T(8,128)S(1)} %bitcast.43) | data formatting | bytes 10485760 | tf_op jit(solution)/shard_map/all_to_all | solution.py:94
  421.4 7.6 %reshape.179 = f32[2048,640]{1,0:T(8,128)} reshape(f32[32,32,2,640]{3,2,1,0:T(2,128)} %bitcast.44) | data formatting | bytes 10485760 | tf_op jit(solution)/shard_map/reshape | solution.py:97
  429.0 11.2 %fusion.15 = f32[1024,640]{0,1:T(8,128)S(1)} fusion(f32[2048,640]{1,0:T(8,128)} %reshape.179, s32[1024]{0:T(1024)S(1)} %bitcast.52), kind=kOutput, calls=%fused_computation.18 | convolution fusion | flops 16108224512 | bytes 7868416 | tf_op jit(solution)/shard_map/dot_general | solution.py:30
  443.1 39.5 %all-reduce.4.cloned.1.call-done = f32[1024,32]{0,1:T(8,128)} async-done(((f32[1024,32]{0,1:T(8,128)}), f32[1024,32]{0,1:T(8,128)}) %all-reduce.4.cloned.1.call-update) | async-done | bytes 131088 | tf_op jit(solution)/shard_map/psum | solution.py:101
  483.8 12.8 %all-gather = f32[4096,32]{0,1:T(8,128)S(1)} all-gather(f32[1024,32]{0,1:T(8,128)S(1)} %multiply_reduce_fusion), channel_id=2, replica_groups=mesh['rows'=32,'rep'=4] {'rep'}, dimensions={0}, use_global_device_ids=true | all-gather | bytes 655360 | tf_op jit(solution)/shard_map/all_gather | solution.py:103
  (199 shorter events, 161.4 us)
Async XLA Ops:
  11.5 247.1 %all-to-all-start.1 = ((f32[32,32,2]{1,2,0:T(2,128)}), f32[32,32,2]{1,2,0:T(2,128)S(1)}, u32[]{:S(2)}, u32[]{:S(2)}) async-start(f32[32,32,2]{1,2,0:T(2,128)} %copy.28), calls=%async_computation.1 | async-start | bytes 65536 | tf_op jit(solution)/shard_map/all_to_all | solution.py:91
  258.7 7.8 %copy-start.1 = (f32[32,4]{0,1:T(4,128)S(1)}, f32[32,4]{0,1:T(4,128)}, u32[]{:S(2)}) copy-start(f32[32,4]{0,1:T(4,128)} %param.12) | copy-start | bytes 1540
  258.7 7.8 %copy-start = (f32[32,8]{0,1:T(8,128)S(1)}, f32[32,8]{0,1:T(8,128)}, u32[]{:S(2)}) copy-start(f32[32,8]{0,1:T(8,128)} %param.13) | copy-start | bytes 3076
  258.7 73.4 %all-to-all-start = ((f32[1024,2,640]{2,1,0:T(2,128)}), f32[1024,2,640]{2,1,0:T(2,128)}, u32[]{:S(2)}, u32[]{:S(2)}) async-start(f32[1024,2,640]{2,1,0:T(2,128)} %reshape.177), calls=%async_computation | async-start | bytes 10485760 | tf_op jit(solution)/shard_map/all_to_all | solution.py:90
  266.1 216.4 %all-reduce.4.cloned.1.call-start = ((), (), s32[]{:S(2)}) async-start(), calls=%async_computation.3 | async-start | bytes 262144 | tf_op jit(solution)/shard_map/psum | solution.py:101
Sparse Core Ops, SparseCore 0:
  441.1 41.3 all-reduce.3
